TPU v7x, 32 devices: a whole 2x2x4 slice. The times are simulated.
32 devices in a mesh: grp: 2 (over y), cell: 8 (over z, x), gene: 2 (over core).
Axes of the slice: x: 2, y: 2, z: 4, core: 2. Of those that a mesh axis runs over, the one named last changes fastest.
Arguments:
- expression: bfloat16 [2048, 16384], P(('grp', 'cell'), 'gene'), parts along dimension 0, may hold values from -6 to 6
- design: bfloat16 [2048, 128], P(('grp', 'cell')), parts along dimension 0, may hold values from -24 to 24
- quantile_level: float32 [16384], P('gene'), may hold values from 0.1 to 0.9
Outputs:
- quantile_slack: bfloat16 [2048, 16384], P(('grp', 'cell'), 'gene'), parts along dimension 0
- low_rank_coef: float32 [32768, 128], P(('grp', 'gene', 'cell')), parts along dimension 0
There are 2 independent parts, one for each index of `grp`. A program takes and returns all parts, laid end to end along the dimension named above; an argument that names none is the same for every part. Nothing has to cross between parts.
All inputs are finite; a program needn't handle non-finite values.
Results may differ from a plain program's by a relative error of at most 0.0025.
The roundings to bfloat16 on the way count: a program that leaves them out, or rounds other values in their place, can miss the bound.
Values may be sent and summed in bfloat16 or wider, within the bound.
No kernel may reach another device: no remote copies, remote signals or barrier semaphores. Data moves between devices by JAX's collectives and lax.ppermute only.
A program may use at most 64 MiB of HBM per device.

v0:
```python
import math
import jax
import jax.numpy as jnp
from jax import lax
from jax.sharding import PartitionSpec as P

NS_STEPS = 8
shrink_rate = 0.25


def matmul(left, right):
    return jnp.dot(left, right, precision=lax.Precision.HIGHEST)


def invert(matrix):
    identity = jnp.eye(matrix.shape[0], dtype=jnp.float32)
    factor = jnp.linalg.cholesky(matrix)
    lower_inv = lax.linalg.triangular_solve(factor, identity, left_side=True, lower=True)
    return matmul(lower_inv.T, lower_inv)


def newton(moment):
    identity = jnp.eye(moment.shape[0], dtype=jnp.float32)
    current = moment / jnp.trace(moment)
    root_inv = identity
    for sweep in range(NS_STEPS):
        middle = 1.5 * identity - 0.5 * matmul(root_inv, current)
        current = matmul(current, middle)
        root_inv = matmul(middle, root_inv)
    return root_inv


def per_device(expression, design, quantile_level):
    width = design.shape[1]
    identity = jnp.eye(width, dtype=jnp.float32)
    local_gram = lax.dot_general(
        design, design, (((0,), (0,)), ((), ())), preferred_element_type=jnp.float32
    )
    crossed = lax.psum_scatter(
        lax.dot_general(
            expression, design, (((0,), (0,)), ((), ())), preferred_element_type=jnp.float32
        ),
        "cell",
        scatter_dimension=0,
        tiled=True,
    )
    gram_total = lax.psum(local_gram, "cell")
    inverse = invert(gram_total + identity)
    coef = matmul(crossed, inverse)
    local_moment = lax.dot_general(
        coef, coef, (((0,), (0,)), ((), ())), precision=lax.Precision.HIGHEST
    )
    moment = lax.psum(local_moment, ("cell", "gene"))
    root_inv = newton(moment)
    low_rank_coef = coef - shrink_rate / math.sqrt(width) * matmul(coef, root_inv)
    coef_low = coef.astype(jnp.bfloat16)
    fitted = lax.dot_general(
        design,
        lax.all_gather(coef_low, "cell", axis=0, tiled=True),
        (((1,), (1,)), ((), ())),
        preferred_element_type=jnp.float32,
    )
    slack = expression.astype(jnp.float32) - fitted
    level = quantile_level[None, :]
    quantile_slack = (slack - jnp.clip(slack, level - 1.0, level)).astype(jnp.bfloat16)
    return (quantile_slack, low_rank_coef)


def solution(mesh):
    placed = (P(("grp", "cell"), "gene"), P(("grp", "cell"), None), P("gene"))
    return jax.shard_map(
        per_device,
        mesh=mesh,
        in_specs=placed,
        out_specs=(P(("grp", "cell"), "gene"), P(("grp", "gene", "cell"), None)),
        check_vma=False,
    )
```

profile of v0, /device:TPU:0, one launch (start us, length us, event | category | flops | bytes accessed | tf_op | source)
XLA Modules:
  0.0 335.5 jit_solution(2231902465308282045)
XLA Ops:
  7.2 0.7 copy-done
  7.9 0.8 fusion.18
  8.8 4.3 %fusion.17 = f32[8192,128]{1,0:T(8,128)} fusion(bf16[128,8192]{1,0:T(8,128)(2,1)} %param.3, bf16[128,128]{1,0:T(8,128)(2,1)S(1)} %copy-done), kind=kOutput, calls=%fused_computation.38 | convolution fusion | flops 268435456 | bytes 6324224 | tf_op jit(solution)/shard_map/dot_general | solution.py:40
  13.4 70.6 %all-reduce.3.cloned.1.call-done = f32[128,128]{0,1:T(8,128)} async-done(((f32[128,128]{0,1:T(8,128)}), f32[128,128]{0,1:T(8,128)}) %all-reduce.3.cloned.1.call-update) | async-done | bytes 65552 | tf_op jit(solution)/shard_map/psum | solution.py:47
  84.0 0.8 convert_add_fusion
  84.9 11.7 %cholesky.29 = f32[128,128]{1,0:T(8,128)S(1)} custom-call(f32[128,128]{1,0:T(8,128)S(1)} %fusion.13), custom_call_target="Cholesky" | custom-call | tf_op jit(solution)/shard_map/jit(cholesky)/cholesky | solution.py:17
  96.7 0.6 compare_reduce_fusion
  97.3 0.7 fusion.10
  98.0 9.8 %custom-call.6 = f32[1,128,128]{1,2,0:T(8,128)S(1)} custom-call(f32[1,128,128]{2,1,0:T(8,128)S(1)} %fusion.10), custom_call_target="InvertDiagBlocksLowerTriangular" | custom-call | tf_op jit(solution)/shard_map/triangular_solve | solution.py:18
  107.8 0.2 fusion.11
  108.0 0.3 fusion.19
  108.3 67.6 %reduce-scatter.2.cloned.1.call-done = f32[1024,128]{1,0:T(8,128)} async-done(((f32[8192,128]{1,0:T(8,128)}), f32[1024,128]{1,0:T(8,128)}) %reduce-scatter.2.cloned.1.call-update) | async-done | bytes 524304 | tf_op jit(solution)/shard_map/reduce_scatter | solution.py:39
  176.0 2.3 fusion.16
  178.3 1.6 fusion.20
  180.0 0.2 all-gather.2.cloned.1.call-start
  180.2 2.4 copy.5
  182.7 83.3 %all-reduce.5.cloned.1.call-done = f32[128,128]{1,0:T(8,128)} async-done(((f32[128,128]{1,0:T(8,128)}), f32[128,128]{1,0:T(8,128)}) %all-reduce.5.cloned.1.call-update) | async-done | bytes 65552 | tf_op jit(solution)/shard_map/psum | solution.py:53
  266.0 1.5 select_reduce_fusion
  267.5 1.7 fusion.9
  269.3 1.7 fusion.15
  275.3 1.4 fusion.1
  276.6 42.0 %all-gather.2.cloned.1.call-done = bf16[8192,128]{1,0:T(8,128)(2,1)} async-done(((bf16[1024,128]{1,0:T(8,128)(2,1)}), bf16[8192,128]{1,0:T(8,128)(2,1)}) %all-gather.2.cloned.1.call-update) | async-done | bytes 2097168 | tf_op jit(solution)/shard_map/all_gather | solution.py:59
  318.7 6.2 %subtract_convert_fusion = bf16[128,8192]{0,1:T(8,128)(2,1)} fusion(bf16[8192,128]{1,0:T(8,128)(2,1)} %all-gather.2.cloned.1.call-done, bf16[128,128]{1,0:T(8,128)(2,1)S(1)} %copy-done, bf16[128,8192]{0,1:T(8,128)(2,1)S(1)} %copy-done.2, f32[8192]{0:T(1024)S(1)} %broadcast_add_fusion, f32[8192]{0:T(1024)S(1)} %copy-done.3), kind=kOutput, calls=%fused_computation.2 | convolution fusion | flops 274726912 | bytes 6389760 | tf_op jit(solution)/shard_map/dot_general | solution.py:57
  324.9 4.1 %copy.9 = bf16[128,8192]{1,0:T(8,128)(2,1)} copy(bf16[128,8192]{0,1:T(8,128)(2,1)} %subtract_convert_fusion) | data formatting | bytes 4194304
  (41 shorter events, 4.8 us)
Async XLA Ops:
  7.2 0.8 copy-start
  7.2 76.8 %all-reduce.3.cloned.1.call-start = ((), (), s32[]{:S(2)}) async-start(), calls=%async_computation.2 | async-start | bytes 131072 | tf_op jit(solution)/shard_map/psum | solution.py:47
  8.8 167.2 %reduce-scatter.2.cloned.1.call-start = ((), (), s32[]{:S(2)}) async-start(), calls=%async_computation.1 | async-start | bytes 4718592 | tf_op jit(solution)/shard_map/reduce_scatter | solution.py:39
  13.1 167.0 %copy-start.3 = (f32[8192]{0:T(1024)S(1)}, f32[8192]{0:T(1024)}, u32[]{:S(2)}) copy-start(f32[8192]{0:T(1024)} %param.5) | copy-start | bytes 98308
  13.2 167.1 %copy-start.1 = (bf16[128,8192]{1,0:T(8,128)(2,1)S(1)}, bf16[128,8192]{1,0:T(8,128)(2,1)}, u32[]{:S(2)}) copy-start(bf16[128,8192]{1,0:T(8,128)(2,1)} %param.3) | copy-start | bytes 6291460
  13.2 252.8 %all-reduce.5.cloned.1.call-start = ((), (), s32[]{:S(2)}) async-start(), calls=%async_computation.4 | async-start | bytes 131072 | tf_op jit(solution)/shard_map/psum | solution.py:53
  180.0 138.7 %all-gather.2.cloned.1.call-start = ((), (), s32[]{:S(2)}) async-start(), calls=%async_computation.3 | async-start | bytes 2359296 | tf_op jit(solution)/shard_map/all_gather | solution.py:59
  271.9 46.8 %copy-start.2 = (bf16[128,8192]{0,1:T(8,128)(2,1)S(1)}, bf16[128,8192]{0,1:T(8,128)(2,1)}, u32[]{:S(2)}) copy-start(bf16[128,8192]{0,1:T(8,128)(2,1)} %copy.5) | copy-start | bytes 6291460
Sparse Core Ops, SparseCore 0:
  12.0 71.9 all-reduce.2
  87.6 88.3 reduce-scatter.1
  180.1 85.8 all-reduce.4
  268.0 50.6 all-gather.1
where the time goes:
time: 336 us; the launch traced here: 335 us
  waiting for transfers between devices  264 us (79%)
  other arithmetic  25.2 us (8%)
  matrix products  24.8 us (7%)
  between operations  14 us (4%)
  local copies, waits for them, and re-layouts  7.44 us (2%)
    psum x1, waiting for transfers between devices, per_device(): moment = lax.psum(local_moment, ('cell', 'gene'))  83.3 us
    psum x1, waiting for transfers between devices, per_device(): gram_total = lax.psum(local_gram, 'cell')  70.6 us
    reduce_scatter x1, waiting for transfers between devices, per_device(): lax.psum_scatter(lax.dot_general(expression, design, (((0,), (0,)), ((),...  67.6 us
    all_gather x1, waiting for transfers between devices, per_device(): lax.all_gather(coef_low, 'cell', axis=0, tiled=True)  42 us
    another operation x4, other arithmetic, invert(): factor = jnp.linalg.cholesky(matrix)  12.4 us
    dot_general x26, matrix products, matmul(): return jnp.dot(left, right, precision=lax.Precision.HIGHEST)  11.6 us
    another operation x2, other arithmetic, invert(): lax.linalg.triangular_solve(factor, identity, left_side=True, lower=True)  10.5 us
    unnamed x10, local copies, waits for them, and re-layouts  7.23 us
  transfers between devices with their start and end apart: 4, of which 4 were waited for; matrix products, arithmetic and copies ran while one was open for 12% of the time, Pallas kernels for 0%

commit v1 on v0

--- a/solution.py
+++ b/solution.py
@@ -6,6 +6,19 @@
 
 NS_STEPS = 8
 shrink_rate = 0.25
+
+
+def gather_around(value, axis, dim):
+    ways = lax.axis_size(axis)
+    up = [(d, (d + 1) % ways) for d in range(ways)]
+    down = [(d, (d - 1) % ways) for d in range(ways)]
+    earlier, later = ([value], [value])
+    for _ in range(ways // 2):
+        earlier.append(lax.ppermute(earlier[-1], axis, up))
+    for _ in range((ways - 1) // 2):
+        later.append(lax.ppermute(later[-1], axis, down))
+    line = jnp.concatenate([*earlier[::-1], *later[1:]], axis=dim)
+    return jnp.roll(line, (lax.axis_index(axis) - ways // 2) * value.shape[dim], axis=dim)
 
 
 def matmul(left, right):
@@ -56,7 +69,7 @@
     coef_low = coef.astype(jnp.bfloat16)
     fitted = lax.dot_general(
         design,
-        lax.all_gather(coef_low, "cell", axis=0, tiled=True),
+        gather_around(coef_low, "cell", 0),
         (((1,), (1,)), ((), ())),
         preferred_element_type=jnp.float32,
     )

time: 336 us -> 330 us (0.982)
  waiting for transfers between devices: 264 us -> 243 us
  starting transfers between devices: 0.34 us -> 17.5 us
    all_gather x1 -> x0, waiting for transfers between devices: 42 us -> none  [per_device(): lax.all_gather(coef_low, 'cell', axis=0, tiled=True)]
    ppermute x0 -> x7, waiting for transfers between devices: none -> 22 us  [the longest x4 19.6 us: gather_around(): earlier.append(lax.ppermute(earlier[-1], axis, up))]
    ppermute x0 -> x7, starting transfers between devices: none -> 17.4 us  [the longest x3 12.8 us: gather_around(): later.append(lax.ppermute(later[-1], axis, down))]
    unnamed x10 -> x25, local copies, waits for them, and re-layouts: 7.23 us -> 6.58 us
  transfers between devices with their start and end apart: 4 -> 10, of which waited for: 4 -> 7; matrix products, arithmetic and copies ran while one was open for 12% -> 13% of each run, Pallas kernels for 0% -> 0%
where the time goes in v1:
time: 330 us; the launch traced here: 329 us
  waiting for transfers between devices  243 us (74%)
  other arithmetic  25.2 us (8%)
  matrix products  22.9 us (7%)
  starting transfers between devices  17.5 us (5%)
  between operations  14.2 us (4%)
  local copies, waits for them, and re-layouts  6.82 us (2%)
    psum x1, waiting for transfers between devices, per_device(): moment = lax.psum(local_moment, ('cell', 'gene'))  82.4 us
    psum x1, waiting for transfers between devices, per_device(): gram_total = lax.psum(local_gram, 'cell')  70.6 us
    reduce_scatter x1, waiting for transfers between devices, per_device(): lax.psum_scatter(lax.dot_general(expression, design, (((0,), (0,)), ((),...  67.6 us
    ppermute x4, waiting for transfers between devices, gather_around(): earlier.append(lax.ppermute(earlier[-1], axis, up))  19.6 us
    ppermute x3, starting transfers between devices, gather_around(): later.append(lax.ppermute(later[-1], axis, down))  12.8 us
    another operation x4, other arithmetic, invert(): factor = jnp.linalg.cholesky(matrix)  12.4 us
    dot_general x26, matrix products, matmul(): return jnp.dot(left, right, precision=lax.Precision.HIGHEST)  10.9 us
    another operation x2, other arithmetic, invert(): lax.linalg.triangular_solve(factor, identity, left_side=True, lower=True)  10.5 us
  transfers between devices with their start and end apart: 10, of which 7 were waited for; matrix products, arithmetic and copies ran while one was open for 13% of the time, Pallas kernels for 0%

profile of v1, /device:TPU:0, one launch (start us, length us, event | category | flops | bytes accessed | tf_op | source)
XLA Modules:
  0.0 329.3 jit_solution(4513608472569050240)
XLA Ops:
  8.8 4.3 %fusion.19 = f32[8192,128]{1,0:T(8,128)} fusion(bf16[128,8192]{1,0:T(8,128)(2,1)} %param.3, bf16[128,128]{1,0:T(8,128)(2,1)S(1)} %copy-done), kind=kOutput, calls=%fused_computation.56 | convolution fusion | flops 268435456 | bytes 6324224 | tf_op jit(solution)/shard_map/dot_general | solution.py:53
  13.4 70.6 %all-reduce.3.cloned.1.call-done = f32[128,128]{0,1:T(8,128)} async-done(((f32[128,128]{0,1:T(8,128)}), f32[128,128]{0,1:T(8,128)}) %all-reduce.3.cloned.1.call-update) | async-done | bytes 65552 | tf_op jit(solution)/shard_map/psum | solution.py:60
  84.9 11.7 %cholesky.29 = f32[128,128]{1,0:T(8,128)S(1)} custom-call(f32[128,128]{1,0:T(8,128)S(1)} %fusion.14), custom_call_target="Cholesky" | custom-call | tf_op jit(solution)/shard_map/jit(cholesky)/cholesky | solution.py:30
  98.0 9.8 %custom-call.6 = f32[1,128,128]{1,2,0:T(8,128)S(1)} custom-call(f32[1,128,128]{2,1,0:T(8,128)S(1)} %fusion.11), custom_call_target="InvertDiagBlocksLowerTriangular" | custom-call | tf_op jit(solution)/shard_map/triangular_solve | solution.py:31
  108.3 67.6 %reduce-scatter.2.cloned.1.call-done = f32[1024,128]{1,0:T(8,128)} async-done(((f32[8192,128]{1,0:T(8,128)}), f32[1024,128]{1,0:T(8,128)}) %reduce-scatter.2.cloned.1.call-update) | async-done | bytes 524304 | tf_op jit(solution)/shard_map/reduce_scatter | solution.py:52
  175.9 1.6 fusion.18
  177.5 1.6 fusion.22
  179.3 2.4 copy.5
  181.7 1.5 collective-permute-start
  183.2 3.2 collective-permute-start.4
  186.4 82.4 %all-reduce.5.cloned.1.call-done = f32[128,128]{1,0:T(8,128)} async-done(((f32[128,128]{1,0:T(8,128)}), f32[128,128]{1,0:T(8,128)}) %all-reduce.5.cloned.1.call-update) | async-done | bytes 65552 | tf_op jit(solution)/shard_map/psum | solution.py:66
  268.8 1.5 select_reduce_fusion
  270.2 1.7 fusion.10
  272.1 1.7 fusion.16
  278.5 9.7 %collective-permute-done.1 = bf16[1024,128]{1,0:T(8,128)(2,1)S(1)} collective-permute-done((bf16[1024,128]{1,0:T(8,128)(2,1)S(1)}, bf16[1024,128]{1,0:T(8,128)(2,1)S(1)}, u32[]{:S(2)}, u32[]{:S(2)}) %collective-permute-start.1) | collective-permute-done | bytes 262176 | tf_op jit(solution)/shard_map/ppermute | solution.py:17
  288.6 4.8 %collective-permute-start.5 = (bf16[1024,128]{1,0:T(8,128)(2,1)S(1)}, bf16[1024,128]{1,0:T(8,128)(2,1)S(1)}, u32[]{:S(2)}, u32[]{:S(2)}) collective-permute-start(bf16[1024,128]{1,0:T(8,128)(2,1)S(1)} %collective-permute-done.4), channel_id=1, source_target_pairs={{0,14},{2,0},{4,2},{6,4},{8,6},{10,8},{12,10},{14,12},{1,15},{3,1}... | collective-permute-start | bytes 786440 | tf_op jit(solution)/shard_map/ppermute | solution.py:19
  293.4 4.9 %collective-permute-done.2 = bf16[1024,128]{1,0:T(8,128)(2,1)S(1)} collective-permute-done((bf16[1024,128]{1,0:T(8,128)(2,1)S(1)}, bf16[1024,128]{1,0:T(8,128)(2,1)S(1)}, u32[]{:S(2)}, u32[]{:S(2)}) %collective-permute-start.2) | collective-permute-done | bytes 262176 | tf_op jit(solution)/shard_map/ppermute | solution.py:17
  298.3 2.0 collective-permute-start.3
  300.5 1.4 fusion.2
  301.9 4.8 %collective-permute-start.6 = (bf16[1024,128]{1,0:T(8,128)(2,1)S(1)}, bf16[1024,128]{1,0:T(8,128)(2,1)S(1)}, u32[]{:S(2)}, u32[]{:S(2)}) collective-permute-start(bf16[1024,128]{1,0:T(8,128)(2,1)S(1)} %collective-permute-done.5), channel_id=1, source_target_pairs={{0,14},{2,0},{4,2},{6,4},{8,6},{10,8},{12,10},{14,12},{1,15},{3,1}... | collective-permute-start | bytes 786440 | tf_op jit(solution)/shard_map/ppermute | solution.py:19
  306.7 5.0 %collective-permute-done.3 = bf16[1024,128]{1,0:T(8,128)(2,1)S(1)} collective-permute-done((bf16[1024,128]{1,0:T(8,128)(2,1)S(1)}, bf16[1024,128]{1,0:T(8,128)(2,1)S(1)}, u32[]{:S(2)}, u32[]{:S(2)}) %collective-permute-start.3) | collective-permute-done | bytes 262176 | tf_op jit(solution)/shard_map/ppermute | solution.py:17
  312.0 2.4 collective-permute-done.6
  314.8 5.0 %subtract_convert_fusion = bf16[128,8192]{0,1:T(8,128)(2,1)S(1)} fusion(bf16[128,128]{1,0:T(8,128)(2,1)S(1)} %copy-done, bf16[128,8192]{0,1:T(8,128)(2,1)S(1)} %copy-done.2, f32[8192]{0:T(1024)S(1)} %broadcast_add_fusion, f32[8192]{0:T(1024)S(1)} %copy-done.3, bf16[16384,128]{1,0:T(8,128)(2,1)S(1)} %constant_dynamic-update-slice_fusion, s32[]{:T(128)S(6)} %select_n.24), kind=kOutput, calls=%fused_computation.2 | convolution fusion | flops 274726912 | bytes 6389764 | tf_op jit(solution)/shard_map/dot_general | solution.py:70
  319.8 2.9 copy.9
  (68 shorter events, 10.6 us)
Async XLA Ops:
  7.2 0.8 copy-start
  7.2 76.8 %all-reduce.3.cloned.1.call-start = ((), (), s32[]{:S(2)}) async-start(), calls=%async_computation.2 | async-start | bytes 131072 | tf_op jit(solution)/shard_map/psum | solution.py:60
  8.8 167.1 %reduce-scatter.2.cloned.1.call-start = ((), (), s32[]{:S(2)}) async-start(), calls=%async_computation.1 | async-start | bytes 4718592 | tf_op jit(solution)/shard_map/reduce_scatter | solution.py:52
  13.1 166.1 %copy-start.3 = (f32[8192]{0:T(1024)S(1)}, f32[8192]{0:T(1024)}, u32[]{:S(2)}) copy-start(f32[8192]{0:T(1024)} %param.5) | copy-start | bytes 98308
  13.1 166.1 %copy-start.1 = (bf16[128,8192]{1,0:T(8,128)(2,1)S(1)}, bf16[128,8192]{1,0:T(8,128)(2,1)}, u32[]{:S(2)}) copy-start(bf16[128,8192]{1,0:T(8,128)(2,1)} %param.3) | copy-start | bytes 6291460
  13.2 255.6 %all-reduce.5.cloned.1.call-start = ((), (), s32[]{:S(2)}) async-start(), calls=%async_computation.3 | async-start | bytes 131072 | tf_op jit(solution)/shard_map/psum | solution.py:66
  181.7 95.3 %collective-permute-start = (bf16[1024,128]{1,0:T(8,128)(2,1)S(1)}, bf16[1024,128]{1,0:T(8,128)(2,1)S(1)}, u32[]{:S(2)}, u32[]{:S(2)}) collective-permute-start(bf16[1024,128]{1,0:T(8,128)(2,1)S(1)} %get-tuple-element.4), channel_id=1, source_target_pairs={{0,2},{2,4},{4,6},{6,8},{8,10},{10,12},{12,14},{14,0},{1,3},{3,5},... | collective-permute-start | bytes 786440 | tf_op jit(solution)/shard_map/ppermute | solution.py:17
  183.2 105.5 %collective-permute-start.4 = (bf16[1024,128]{1,0:T(8,128)(2,1)S(1)}, bf16[1024,128]{1,0:T(8,128)(2,1)S(1)}, u32[]{:S(2)}, u32[]{:S(2)}) collective-permute-start(bf16[1024,128]{1,0:T(8,128)(2,1)S(1)} %get-tuple-element.4), channel_id=1, source_target_pairs={{0,14},{2,0},{4,2},{6,4},{8,6},{10,8},{12,10},{14,12},{1,15},{3,1}... | collective-permute-start | bytes 786440 | tf_op jit(solution)/shard_map/ppermute | solution.py:19
  277.0 11.2 %collective-permute-start.1 = (bf16[1024,128]{1,0:T(8,128)(2,1)S(1)}, bf16[1024,128]{1,0:T(8,128)(2,1)S(1)}, u32[]{:S(2)}, u32[]{:S(2)}) collective-permute-start(bf16[1024,128]{1,0:T(8,128)(2,1)S(1)} %collective-permute-done), channel_id=1, source_target_pairs={{0,2},{2,4},{4,6},{6,8},{8,10},{10,12},{12,14},{14,0},{1,3},{3,5},... | collective-permute-start | bytes 786440 | tf_op jit(solution)/shard_map/ppermute | solution.py:17
  288.2 10.1 %collective-permute-start.2 = (bf16[1024,128]{1,0:T(8,128)(2,1)S(1)}, bf16[1024,128]{1,0:T(8,128)(2,1)S(1)}, u32[]{:S(2)}, u32[]{:S(2)}) collective-permute-start(bf16[1024,128]{1,0:T(8,128)(2,1)S(1)} %collective-permute-done.1), channel_id=1, source_target_pairs={{0,2},{2,4},{4,6},{6,8},{8,10},{10,12},{12,14},{14,0},{1,3},{3,5},... | collective-permute-start | bytes 786440 | tf_op jit(solution)/shard_map/ppermute | solution.py:17
  288.6 13.3 %collective-permute-start.5 = (bf16[1024,128]{1,0:T(8,128)(2,1)S(1)}, bf16[1024,128]{1,0:T(8,128)(2,1)S(1)}, u32[]{:S(2)}, u32[]{:S(2)}) collective-permute-start(bf16[1024,128]{1,0:T(8,128)(2,1)S(1)} %collective-permute-done.4), channel_id=1, source_target_pairs={{0,14},{2,0},{4,2},{6,4},{8,6},{10,8},{12,10},{14,12},{1,15},{3,1}... | collective-permute-start | bytes 786440 | tf_op jit(solution)/shard_map/ppermute | solution.py:19
  298.3 13.4 %collective-permute-start.3 = (bf16[1024,128]{1,0:T(8,128)(2,1)S(1)}, bf16[1024,128]{1,0:T(8,128)(2,1)S(1)}, u32[]{:S(2)}, u32[]{:S(2)}) collective-permute-start(bf16[1024,128]{1,0:T(8,128)(2,1)S(1)} %collective-permute-done.2), channel_id=1, source_target_pairs={{0,2},{2,4},{4,6},{6,8},{8,10},{10,12},{12,14},{14,0},{1,3},{3,5},... | collective-permute-start | bytes 786440 | tf_op jit(solution)/shard_map/ppermute | solution.py:17
  301.9 12.9 %copy-start.2 = (bf16[128,8192]{0,1:T(8,128)(2,1)S(1)}, bf16[128,8192]{0,1:T(8,128)(2,1)}, u32[]{:S(2)}) copy-start(bf16[128,8192]{0,1:T(8,128)(2,1)} %copy.5) | copy-start | bytes 6291460
  301.9 12.5 %collective-permute-start.6 = (bf16[1024,128]{1,0:T(8,128)(2,1)S(1)}, bf16[1024,128]{1,0:T(8,128)(2,1)S(1)}, u32[]{:S(2)}, u32[]{:S(2)}) collective-permute-start(bf16[1024,128]{1,0:T(8,128)(2,1)S(1)} %collective-permute-done.5), channel_id=1, source_target_pairs={{0,14},{2,0},{4,2},{6,4},{8,6},{10,8},{12,10},{14,12},{1,15},{3,1}... | collective-permute-start | bytes 786440 | tf_op jit(solution)/shard_map/ppermute | solution.py:19
Sparse Core Ops, SparseCore 0:
  12.0 71.9 all-reduce.2
  87.6 88.2 reduce-scatter.1
  180.0 88.7 all-reduce.4
